TPU v7x, 512 devices: a whole 4x4x16 slice. The times are simulated.
512 devices in a mesh: row: 32 (over z_lo, x), col: 16 (over y, z_hi, core).
Axes of the slice: x: 4, y: 4, z: 16 (z_hi: 2, z_lo: 8; z = z_hi * 8 + z_lo), core: 2. Of those that a mesh axis runs over, the one named last changes fastest.
Arguments:
- anc_inv: bfloat16 [16384, 16384], P('row', 'col'), may hold values from -0.0546875 to 0.0546875
- panel: bfloat16 [1, 12288, 2048], P(None, 'col', 'row'), may hold values from -6 to 6
- structure: int32 [1, 96], replicated, may hold values from 0 to 127, as said below
Outputs:
- off_inv: float32 [1, 16384, 2048], P(None, 'row', 'col')
Inputs may be any that keep to these rules, and one draw needn't show every extreme that they name: Each structure[s] holds 96 distinct ancestor block indices, in the order in which the panel stores its row blocks (not sorted); each group of 8 consecutive ancestor blocks holds 5 to 7 of them, and some group of each supernode holds exactly 7.
All inputs are finite; a program needn't handle non-finite values.
Results may differ from a plain program's by a relative error of at most 0.0003.
Values may be sent and summed in bfloat16 or wider, within the bound.
No kernel may reach another device: no remote copies, remote signals or barrier semaphores. Data moves between devices by JAX's collectives and lax.ppermute only.
A program may use at most 64 MiB of HBM per device.

v0:
```python
import jax
import jax.numpy as jnp
from jax import lax
from jax.sharding import PartitionSpec as P

BS = 128
SBLK = 96


def body(anc_inv, panel, structure):
    col_index = lax.axis_index("col")
    row_index = lax.axis_index("row")
    local_rows, local_cols = anc_inv.shape
    group_blocks = local_cols // BS
    local_width = panel.shape[2]
    gathered = lax.all_gather(panel, "col", axis=1, tiled=True)
    own_blocks = row_index * (local_rows // BS) + jnp.arange(local_rows // BS, dtype=jnp.int32)
    block_ids = jnp.arange(group_blocks, dtype=jnp.int32)
    blocks_of = structure[0]
    compact = gathered[0].reshape(SBLK, BS * local_width)
    local_block = blocks_of - col_index * group_blocks
    picker = (local_block[None, :] == block_ids[:, None]).astype(jnp.bfloat16)
    picked = (
        jnp.dot(picker, compact, preferred_element_type=jnp.float32)
        .astype(jnp.bfloat16)
        .reshape(group_blocks * BS, local_width)
    )
    partial_value = jnp.dot(
        anc_inv,
        lax.all_gather(picked, "row", axis=1, tiled=True),
        preferred_element_type=jnp.float32,
    )
    summed = lax.psum_scatter(partial_value, "col", scatter_dimension=1, tiled=True)
    member = jnp.any(blocks_of[None, :] == own_blocks[:, None], axis=1)
    row_mask = jnp.repeat(member, BS)
    results = [jnp.where(row_mask[:, None], -summed, jnp.zeros_like(summed))]
    return jnp.stack(results)


def solution(mesh):
    in_specs = (P("row", "col"), P(None, "col", "row"), P())
    out_specs = P(None, "row", "col")
    return jax.shard_map(body, mesh=mesh, in_specs=in_specs, out_specs=out_specs, check_vma=False)
```

profile of v0, /device:TPU:2, one launch (start us, length us, event | category | flops | bytes accessed | tf_op | source)
XLA Modules:
  0.0 496.0 jit_solution(13682171453870324515)
XLA Ops:
  6.5 0.0 copy-start
  6.5 0.0 all-gather.3.cloned.1.call-start
  6.5 0.7 all-gather.3.cloned.1.call-update
  7.3 0.0 all-gather.5.cloned.1.call-start
  7.3 0.7 subtract_bitcast_fusion
  8.0 92.1 %all-gather.3.cloned.1.call-done = bf16[1,12288,64]{1,2,0:T(8,128)(2,1)} async-done(((bf16[1,768,64]{1,2,0:T(8,128)(2,1)}), bf16[1,12288,64]{1,2,0:T(8,128)(2,1)}) %all-gather.3.cloned.1.call-update) | async-done | bytes 1572880 | tf_op jit(solution)/shard_map/all_gather | solution.py:16
  100.1 4.1 copy.10
  104.2 4.3 reshape_squeeze.3
  108.4 0.3 convolution_convert_fusion
  108.7 0.3 reshape.8
  109.0 0.8 copy.11
  109.8 0.0 all-gather.5.cloned.1.call-update
  109.8 0.0 reduce-scatter.2.cloned.1.call-start
  109.9 218.6 %all-gather.5.cloned.1.call-done = bf16[1024,2048]{0,1:T(8,128)(2,1)} async-done(((bf16[1024,64]{0,1:T(8,128)(2,1)}), bf16[1024,2048]{0,1:T(8,128)(2,1)}) %all-gather.5.cloned.1.call-update) | async-done | bytes 4194320 | tf_op jit(solution)/shard_map/all_gather | solution.py:30
  328.5 0.0 copy-done
  328.5 6.5 %convolution_bitcast_fusion = f32[512,2048]{0,1:T(8,128)} fusion(bf16[1024,2048]{0,1:T(8,128)(2,1)} %all-gather.5.cloned.1.call-done, bf16[512,1024]{1,0:T(8,128)(2,1)S(1)} %copy-done), kind=kOutput, calls=%fused_computation.1 | convolution fusion | flops 2147483648 | bytes 9437184 | tf_op jit(solution)/shard_map/dot_general | solution.py:28
  335.0 0.0 copy-start.1
  335.0 0.0 reduce-scatter.2.cloned.1.call-update
  335.0 0.6 copy-done.1
  335.6 0.2 compare_reduce_fusion
  335.8 0.1 broadcast_bitcast_fusion
  335.9 151.7 %reduce-scatter.2.cloned.1.call-done = f32[512,128]{0,1:T(8,128)} async-done(((f32[512,2048]{0,1:T(8,128)}), f32[512,128]{0,1:T(8,128)}) %reduce-scatter.2.cloned.1.call-update) | async-done | bytes 262160 | tf_op jit(solution)/shard_map/reduce_scatter | solution.py:33
  487.6 1.0 select_bitcast_fusion
  488.6 0.8 copy.12
  (1 shorter events, 0.0 us)
Async XLA Ops:
  6.5 321.9 %copy-start = (bf16[512,1024]{1,0:T(8,128)(2,1)S(1)}, bf16[512,1024]{1,0:T(8,128)(2,1)}, u32[]{:S(2)}) copy-start(bf16[512,1024]{1,0:T(8,128)(2,1)} %param.3) | copy-start | bytes 3145732
  6.5 93.5 %all-gather.3.cloned.1.call-start = ((), (), s32[]{:S(2)}) async-start(), calls=%async_computation.1 | async-start | bytes 1671168 | tf_op jit(solution)/shard_map/all_gather | solution.py:16
  7.3 321.2 %all-gather.5.cloned.1.call-start = ((), (), s32[]{:S(2)}) async-start(), calls=%async_computation.2 | async-start | bytes 4325376 | tf_op jit(solution)/shard_map/all_gather | solution.py:30
  109.8 377.8 %reduce-scatter.2.cloned.1.call-start = ((), (), s32[]{:S(2)}) async-start(), calls=%async_computation.3 | async-start | bytes 4456448 | tf_op jit(solution)/shard_map/reduce_scatter | solution.py:33
  335.0 0.7 copy-start.1
Sparse Core Ops, SparseCore 0:
  10.6 89.3 all-gather.2
  109.9 218.4 all-gather.4
  335.1 152.4 reduce-scatter.1
where the time goes:
time: 496 us
  waiting for transfers between devices  463 us (93%)
  between operations  13.2 us (3%)
  local copies, waits for them, and re-layouts  11 us (2%)
  matrix products  6.81 us (1%)
    all_gather x1, waiting for transfers between devices, body(): lax.all_gather(picked, 'row', axis=1, tiled=True)  219 us
    reduce_scatter x1, waiting for transfers between devices, body(): lax.psum_scatter(partial_value, 'col', scatter_dimension=1, tiled=True)  152 us
    all_gather x1, waiting for transfers between devices, body(): gathered = lax.all_gather(panel, 'col', axis=1, tiled=True)  92.1 us
  transfers between devices with their start and end apart: 3, of which 3 were waited for; matrix products, arithmetic and copies ran while one was open for 0% of the time, Pallas kernels for 0%

commit v1 on v0

--- a/solution.py
+++ b/solution.py
@@ -5,6 +5,11 @@
 
 BS = 128
 SBLK = 96
+
+
+def all_by_exchange(x, axis, along):
+    sent = jnp.stack([x] * lax.axis_size(axis))
+    return jnp.concatenate(lax.all_to_all(sent, axis, 0, 0), axis=along)
 
 
 def body(anc_inv, panel, structure):
@@ -26,9 +31,7 @@
         .reshape(group_blocks * BS, local_width)
     )
     partial_value = jnp.dot(
-        anc_inv,
-        lax.all_gather(picked, "row", axis=1, tiled=True),
-        preferred_element_type=jnp.float32,
+        anc_inv, all_by_exchange(picked, "row", 1), preferred_element_type=jnp.float32
     )
     summed = lax.psum_scatter(partial_value, "col", scatter_dimension=1, tiled=True)
     member = jnp.any(blocks_of[None, :] == own_blocks[:, None], axis=1)

time: 496 us -> 464 us (0.935)
  waiting for transfers between devices: 463 us -> 242 us
  blocking collectives: 0 us -> 191 us
    all_gather x1 -> x0, waiting for transfers between devices: 219 us -> none  [body(): lax.all_gather(picked, 'row', axis=1, tiled=True)]
    all_to_all x0 -> x1, blocking collectives: none -> 191 us  [all_by_exchange(): return jnp.concatenate(lax.all_to_all(sent, axis, 0, 0), axis=along)]
  transfers between devices with their start and end apart: 3 -> 2, of which waited for: 3 -> 2; matrix products, arithmetic and copies ran while one was open for 0% -> 0% of each run, Pallas kernels for 0% -> 0%
where the time goes in v1:
time: 464 us
  waiting for transfers between devices  242 us (52%)
  blocking collectives  191 us (41%)
  between operations  13.5 us (3%)
  local copies, waits for them, and re-layouts  10.8 us (2%)
  matrix products  4.65 us (1%)
    all_to_all x1, blocking collectives, all_by_exchange(): return jnp.concatenate(lax.all_to_all(sent, axis, 0, 0), axis=along)  191 us
    reduce_scatter x1, waiting for transfers between devices, body(): lax.psum_scatter(partial_value, 'col', scatter_dimension=1, tiled=True)  149 us
    all_gather x1, waiting for transfers between devices, body(): gathered = lax.all_gather(panel, 'col', axis=1, tiled=True)  92.1 us
  transfers between devices with their start and end apart: 2, of which 2 were waited for; matrix products, arithmetic and copies ran while one was open for 0% of the time, Pallas kernels for 0%

profile of v1, /device:TPU:2, one launch (start us, length us, event | category | flops | bytes accessed | tf_op | source)
XLA Modules:
  0.0 463.7 jit_solution(12561558436711246192)
XLA Ops:
  6.5 0.0 copy-start
  6.5 0.0 all-gather.2.cloned.1.call-start
  6.5 0.7 all-gather.2.cloned.1.call-update
  7.3 0.0 reduce-scatter.2.cloned.1.call-start
  7.3 0.7 subtract_bitcast_fusion
  8.0 92.1 %all-gather.2.cloned.1.call-done = bf16[1,12288,64]{1,2,0:T(8,128)(2,1)} async-done(((bf16[1,768,64]{1,2,0:T(8,128)(2,1)}), bf16[1,12288,64]{1,2,0:T(8,128)(2,1)}) %all-gather.2.cloned.1.call-update) | async-done | bytes 1572880 | tf_op jit(solution)/shard_map/all_gather | solution.py:21
  100.1 4.1 copy.8
  104.2 4.3 reshape_squeeze.3
  108.5 0.3 convolution_convert_fusion
  108.8 0.3 stack_reshape.2
  109.0 0.1 copy.9
  109.2 0.5 stack.6
  109.7 191.0 %all_to_all.5 = bf16[32,1024,64]{1,2,0:T(8,128)(2,1)S(1)} all-to-all(bf16[32,1024,64]{1,2,0:T(8,128)(2,1)S(1)} %stack.6), channel_id=1, replica_groups=mesh['row'=32,'col'=16] {'row'}, dimensions={0} | all-to-all | bytes 8388608 | tf_op jit(solution)/shard_map/all_to_all | solution.py:12
  300.7 0.0 copy-done
  300.7 4.3 convolution_bitcast_fusion
  305.0 0.0 copy-start.1
  305.0 0.0 reduce-scatter.2.cloned.1.call-update
  305.1 0.6 copy-done.1
  305.7 0.2 compare_reduce_fusion
  305.9 0.1 broadcast_bitcast_fusion
  305.9 149.1 %reduce-scatter.2.cloned.1.call-done = f32[512,128]{0,1:T(8,128)} async-done(((f32[512,2048]{0,1:T(8,128)}), f32[512,128]{0,1:T(8,128)}) %reduce-scatter.2.cloned.1.call-update) | async-done | bytes 262160 | tf_op jit(solution)/shard_map/reduce_scatter | solution.py:36
  455.1 1.0 select_bitcast_fusion
  456.0 0.8 copy.10
  (1 shorter events, 0.0 us)
Async XLA Ops:
  6.5 294.1 %copy-start = (bf16[512,1024]{1,0:T(8,128)(2,1)S(1)}, bf16[512,1024]{1,0:T(8,128)(2,1)}, u32[]{:S(2)}) copy-start(bf16[512,1024]{1,0:T(8,128)(2,1)} %param.3) | copy-start | bytes 3145732
  6.5 93.5 %all-gather.2.cloned.1.call-start = ((), (), s32[]{:S(2)}) async-start(), calls=%async_computation.2 | async-start | bytes 1671168 | tf_op jit(solution)/shard_map/all_gather | solution.py:21
  7.3 447.8 %reduce-scatter.2.cloned.1.call-start = ((), (), s32[]{:S(2)}) async-start(), calls=%async_computation.3 | async-start | bytes 4456448 | tf_op jit(solution)/shard_map/reduce_scatter | solution.py:36
  305.0 0.7 copy-start.1
Sparse Core Ops, SparseCore 0:
  10.6 89.3 all-gather.1
  305.2 149.8 reduce-scatter.1
